TPU v7x, 512 devices: a whole 4x8x8 slice. The times are simulated.
512 devices in a mesh: gx: 8 (over z), gy: 8 (over y), gz: 8 (over x, core).
Axes of the slice: x: 4, y: 8, z: 8, core: 2. Of those that a mesh axis runs over, the one named last changes fastest.
Arguments:
- reference_image: bfloat16 [128, 128, 1024], P('gx', 'gy', 'gz'), may hold values from -60 to 60
- deformed_image: bfloat16 [128, 128, 1024], P('gx', 'gy', 'gz'), may hold values from -60 to 60
- roi_mask: int32 [128, 128, 1024], P('gx', 'gy', 'gz'), may hold values 0 or 1
- displacement: float32 [3, 32768, 8], P(None, ('gx', 'gy', 'gz')), may hold values from -12 to 12
- node_map: int32 [32768], P(('gx', 'gy', 'gz')), may hold values from 0 to 4095, as said below
Outputs:
- displacement_out: float32 [3, 32768, 8], P(None, ('gx', 'gy', 'gz'))
Inputs may be any that keep to these rules, and one draw needn't show every extreme that they name: Within each slab (devices with one gx index) node_map is a permutation of 0 to 4095. Every device lists exactly 2 blocks of one tile and at most one block of each other tile.
All inputs are finite; a program needn't handle non-finite values. No bound on the sum of `roi_mask` on one device may be relied on, other than what follows from the above.
Results may differ from a plain program's by a relative error of at most 0.00083.
Values may be sent and summed in bfloat16 or wider, within the bound.
No kernel may reach another device: no remote copies, remote signals or barrier semaphores. Data moves between devices by JAX's collectives and lax.ppermute only.
A program may use at most 64 MiB of HBM per device.

v0:
```python
import jax
import jax.numpy as jnp
from jax import lax
from jax.sharding import PartitionSpec as P

ELEM = 4
ITERS = 2
CAP = 2
binomial = (0.0625, 0.25, 0.375, 0.25, 0.0625)
lame_lambda = 1.0
shear_modulus = 0.5
elastic_weight = 2.0
diagonal_shift = 6.0
highest = lax.Precision.HIGHEST


def with_halo(block, sides, width):
    for axis, dim in sides:
        count = lax.axis_size(axis)
        forward = [(i, i + 1) for i in range(count - 1)]
        backward = [(target, source) for source, target in forward]
        low = lax.ppermute(
            lax.slice_in_dim(block, block.shape[dim] - width, None, axis=dim), axis, forward
        )
        high = lax.ppermute(lax.slice_in_dim(block, 0, width, axis=dim), axis, backward)
        block = jnp.concatenate([low, block, high], axis=dim)
    return block


def smooth_axis(volume, dimension):
    length = volume.shape[dimension] - 4
    summed = binomial[0] * lax.slice_in_dim(volume, 0, length, axis=dimension)
    for offset in range(1, 5):
        summed = summed + binomial[offset] * lax.slice_in_dim(
            volume, offset, offset + length, axis=dimension
        )
    return summed


def derive_fields(first_padded, second_padded):
    first_smooth = first_padded
    second_smooth = second_padded
    for dimension in range(3):
        first_smooth = smooth_axis(first_smooth, dimension)
        second_smooth = smooth_axis(second_smooth, dimension)
    average = (first_smooth + second_smooth) * 0.5
    contrast = (second_smooth - first_smooth)[1:-1, 1:-1, 1:-1].astype(jnp.bfloat16)
    slopes = []
    for dimension in range(3):
        length = average.shape[dimension] - 2
        forward_part = lax.slice_in_dim(average, 2, length + 2, axis=dimension)
        backward_part = lax.slice_in_dim(average, 0, length, axis=dimension)
        gradient = (forward_part - backward_part) * 0.5
        for cropped_dim in range(3):
            if cropped_dim != dimension:
                gradient = lax.slice_in_dim(
                    gradient, 1, gradient.shape[cropped_dim] - 1, axis=cropped_dim
                )
        slopes.append(gradient.astype(jnp.bfloat16))
    return jnp.stack([contrast] + slopes)


def interp_axis(volume, dimension, cells_edge):
    length = volume.shape[dimension]
    before = lax.slice_in_dim(volume, 0, length - 1, axis=dimension)
    after = lax.slice_in_dim(volume, 1, length, axis=dimension)
    shape_one = [1] * (volume.ndim + 1)
    shape_one[dimension + 1] = cells_edge
    fraction = (jnp.arange(cells_edge, dtype=jnp.float32) / cells_edge).reshape(shape_one)
    merged = (
        jnp.expand_dims(before, dimension + 1) * (1.0 - fraction)
        + jnp.expand_dims(after, dimension + 1) * fraction
    )
    new_shape = list(volume.shape)
    new_shape[dimension] = (length - 1) * cells_edge
    return merged.reshape(new_shape)


def collect_axis(volume, dimension, cells_edge, squared):
    elements = volume.shape[dimension] // cells_edge
    split_shape = (
        list(volume.shape[:dimension])
        + [elements, cells_edge]
        + list(volume.shape[dimension + 1 :])
    )
    pieces = volume.reshape(split_shape)
    shape_one = [1] * len(split_shape)
    shape_one[dimension + 1] = cells_edge
    fraction = (jnp.arange(cells_edge, dtype=jnp.float32) / cells_edge).reshape(shape_one)
    weight_low = 1.0 - fraction
    weight_high = fraction
    if squared:
        weight_low = weight_low * weight_low
        weight_high = weight_high * weight_high
    low_side = jnp.sum(pieces * weight_low, axis=dimension + 1)
    high_side = jnp.sum(pieces * weight_high, axis=dimension + 1)
    return lax.slice_in_dim(low_side, 1, elements, axis=dimension) + lax.slice_in_dim(
        high_side, 0, elements - 1, axis=dimension
    )


def pair_op(volume, dimension, factor):
    length = volume.shape[dimension]
    return lax.slice_in_dim(volume, 1, length, axis=dimension) + factor * lax.slice_in_dim(
        volume, 0, length - 1, axis=dimension
    )


def cross_pairs(volume, chosen, factor, offset):
    for dimension in range(3):
        volume = pair_op(volume, dimension + offset, factor if dimension == chosen else 1.0)
    return volume


def elastic_force(padded):
    gradients = [cross_pairs(padded, chosen, -1.0, 1) * (1.0 / (4.0 * ELEM)) for chosen in range(3)]
    deform = [
        [gradients[source][target] + (1.0 if target == source else 0.0) for source in range(3)]
        for target in range(3)
    ]
    strain = [
        [
            0.5
            * (
                deform[0][target] * deform[0][source]
                + deform[1][target] * deform[1][source]
                + deform[2][target] * deform[2][source]
            )
            - (0.5 if target == source else 0.0)
            for source in range(3)
        ]
        for target in range(3)
    ]
    trace_strain = strain[0][0] + strain[1][1] + strain[2][2]
    stress = [
        [
            2.0 * shear_modulus * strain[target][source]
            + (lame_lambda * trace_strain if target == source else 0.0)
            for source in range(3)
        ]
        for target in range(3)
    ]
    nominal = [
        [
            deform[target][0] * stress[0][source]
            + deform[target][1] * stress[1][source]
            + deform[target][2] * stress[2][source]
            for source in range(3)
        ]
        for target in range(3)
    ]
    coefficient = ELEM * ELEM / 4.0
    forces = []
    for target in range(3):
        summed = cross_pairs(nominal[target][0], 0, -1.0, 0)
        for source in range(1, 3):
            summed = summed + cross_pairs(nominal[target][source], source, -1.0, 0)
        forces.append(-coefficient * summed)
    return jnp.stack(forces)


def axis_table(nodes_len, cells_edge, squared):
    voxels = (nodes_len - 1) * cells_edge
    column = jnp.arange(voxels, dtype=jnp.int32)
    element = column // cells_edge
    fraction = (column % cells_edge).astype(jnp.float32) / cells_edge
    weight_low = 1.0 - fraction
    weight_high = fraction
    if squared:
        weight_low = weight_low * weight_low
        weight_high = weight_high * weight_high
    node_row = jnp.arange(nodes_len, dtype=jnp.int32)[:, None]
    return jnp.where(node_row == element[None, :], weight_low[None, :], 0.0) + jnp.where(
        node_row == element[None, :] + 1, weight_high[None, :], 0.0
    )


def spread(padded, weights_table):
    shape_all = padded.shape
    stretched = jnp.dot(padded.reshape(-1, shape_all[3]), weights_table, precision=highest)
    stretched = stretched.reshape(shape_all[0], shape_all[1], shape_all[2], weights_table.shape[1])
    stretched = interp_axis(stretched, 1, ELEM)
    return interp_axis(stretched, 2, ELEM)


def collect(volume, table_back, squared):
    shape_all = volume.shape
    reduced = jnp.dot(volume.reshape(-1, shape_all[3]), table_back, precision=highest)
    reduced = reduced.reshape(shape_all[0], shape_all[1], shape_all[2], table_back.shape[1])
    reduced = collect_axis(reduced, 2, ELEM, squared)
    return collect_axis(reduced, 1, ELEM, squared)


def per_device(reference_image, deformed_image, roi_mask, displacement, node_map):
    mask_half = roi_mask.astype(jnp.bfloat16)
    stacked = jnp.stack([reference_image, deformed_image])
    padded_images = with_halo(stacked, (("gx", 1), ("gy", 2), ("gz", 3)), 5)
    derived = derive_fields(
        padded_images[0].astype(jnp.float32), padded_images[1].astype(jnp.float32)
    )
    region = with_halo(mask_half, (("gx", 0), ("gy", 1), ("gz", 2)), 2).astype(jnp.float32)
    contrast = derived[0].astype(jnp.float32)
    slopes = derived[1:].astype(jnp.float32)
    masked_slopes = slopes * region[None]
    nodes_shape = (
        3,
        reference_image.shape[0] // ELEM,
        reference_image.shape[1] // ELEM,
        reference_image.shape[2] // ELEM,
    )
    weights_table = axis_table(nodes_shape[3] + 2, ELEM, False)
    table_back = weights_table[1:-1].T
    table_square = axis_table(nodes_shape[3] + 2, ELEM, True)[1:-1].T
    curvature = collect(masked_slopes * slopes, table_square, True) + diagonal_shift
    members = lax.axis_size(("gy", "gz"))
    blocks = node_map.shape[0]
    block_nodes = displacement.shape[2]
    owner_tile = node_map // blocks
    tile_block = node_map % blocks
    position = jnp.arange(blocks, dtype=jnp.int32)
    earlier = (owner_tile[:, None] == owner_tile[None, :]) & (position[None, :] < position[:, None])
    ranking = jnp.sum(earlier.astype(jnp.int32), axis=1)
    target_slot = owner_tile * CAP + ranking
    packing = (target_slot[:, None] == jnp.arange(members * CAP, dtype=jnp.int32)[None, :]).astype(
        jnp.float32
    )
    labels = jnp.dot((tile_block + 1).astype(jnp.float32), packing, precision=highest).reshape(
        1, members * CAP
    )
    current = displacement
    for iteration in range(ITERS):
        send_channels = current.shape[0]
        send_outgoing = jnp.einsum("cjn,jp->cpn", current, packing, precision=highest).reshape(
            send_channels, -1
        )
        send_incoming = lax.all_to_all(
            send_outgoing, ("gy", "gz"), split_axis=1, concat_axis=1, tiled=True
        )
        received_labels = lax.all_to_all(
            labels, ("gy", "gz"), split_axis=1, concat_axis=1, tiled=True
        )
        send_placing = (
            received_labels.reshape(-1)[:, None] == (position + 1).astype(jnp.float32)[None, :]
        ).astype(jnp.float32)
        send_tile_values = jnp.einsum(
            "cpn,pk->ckn",
            send_incoming.reshape(send_channels, members * CAP, -1),
            send_placing,
            precision=highest,
        )
        padded = with_halo(
            send_tile_values.reshape(nodes_shape), (("gx", 1), ("gy", 2), ("gz", 3)), 1
        )
        moved = spread(padded, weights_table)
        residual = contrast + slopes[0] * moved[0] + slopes[1] * moved[1] + slopes[2] * moved[2]
        image_part = collect(masked_slopes * residual[None], table_back, False)
        force_total = image_part + elastic_weight * elastic_force(padded)
        sums = jnp.concatenate([force_total, curvature]).reshape(6, blocks, block_nodes)
        channels = sums.shape[0]
        outgoing = jnp.einsum("ckn,pk->cpn", sums, send_placing, precision=highest).reshape(
            channels, -1
        )
        incoming = lax.all_to_all(outgoing, ("gy", "gz"), split_axis=1, concat_axis=1, tiled=True)
        returned = jnp.einsum(
            "cpn,jp->cjn", incoming.reshape(channels, members * CAP, -1), packing, precision=highest
        )
        current = current - returned[:3] / returned[3:]
    return current


def solution(mesh):
    in_specs = (
        P("gx", "gy", "gz"),
        P("gx", "gy", "gz"),
        P("gx", "gy", "gz"),
        P(None, ("gx", "gy", "gz"), None),
        P(("gx", "gy", "gz")),
    )
    out_specs = P(None, ("gx", "gy", "gz"), None)
    return jax.shard_map(
        per_device, mesh=mesh, in_specs=in_specs, out_specs=out_specs, check_vma=False
    )
```

profile of v0, /device:TPU:193, one launch (start us, length us, event | category | flops | bytes accessed | tf_op | source)
XLA Modules:
  0.0 224.7 jit_solution(1348251170482457069)
XLA Ops:
  3.1 10.8 %all-to-all-start = ((f32[1,64,2]{2,0,1:T(1,128)}), f32[1,64,2]{2,0,1:T(1,128)S(1)}, u32[]{:S(2)}, u32[]{:S(2)}) async-start(f32[1,64,2]{2,0,1:T(1,128)} %bitcast.2), calls=%async_computation | async-start | bytes 65536 | tf_op jit(solution)/shard_map/all_to_all | solution.py:239
  14.7 5.2 %collective-permute-start = (bf16[2,5,16,128]{3,2,1,0:T(8,128)(2,1)S(1)}, bf16[2,5,16,128]{3,2,1,0:T(8,128)(2,1)S(1)}, u32[]{:S(2)}, u32[]{:S(2)}) collective-permute-start(bf16[2,5,16,128]{3,2,1,0:T(8,128)(2,1)S(1)} %get-tuple-element.88), channel_id=1, source_target_pairs={{0,64},{64,128},{128,192},{192,256},{256,320},{320,384},{384,448},... | collective-permute-start | bytes 122888 | tf_op jit(solution)/shard_map/ppermute | solution.py:22
  20.9 3.1 %collective-permute-start.6 = (bf16[2,16,128]{2,1,0:T(8,128)(2,1)S(1)}, bf16[2,16,128]{2,1,0:T(8,128)(2,1)S(1)}, u32[]{:S(2)}, u32[]{:S(2)}) collective-permute-start(bf16[2,16,128]{2,1,0:T(8,128)(2,1)S(1)} %get-tuple-element.102), channel_id=1, source_target_pairs={{0,64},{64,128},{128,192},{192,256},{256,320},{320,384},{384,448},... | collective-permute-start | bytes 24584 | tf_op jit(solution)/shard_map/ppermute | solution.py:22
  29.7 3.3 %collective-permute-start.8 = (bf16[20,2,128]{2,1,0:T(2,128)(2,1)S(1)}, bf16[20,2,128]{2,1,0:T(2,128)(2,1)S(1)}, u32[]{:S(2)}, u32[]{:S(2)}) collective-permute-start(bf16[20,2,128]{2,1,0:T(2,128)(2,1)S(1)} %get-tuple-element.92), channel_id=1, source_target_pairs={{0,8},{8,16},{16,24},{24,32},{32,40},{40,48},{48,56},{1,9},{9,17},... | collective-permute-start | bytes 30728 | tf_op jit(solution)/shard_map/ppermute | solution.py:22
  35.2 14.4 %all-to-all-start.1 = ((f32[3,64,16]{2,0,1:T(4,128)}), f32[3,64,16]{2,0,1:T(4,128)S(1)}, u32[]{:S(2)}, u32[]{:S(2)}) async-start(f32[3,64,16]{2,0,1:T(4,128)} %copy.112), calls=%async_computation.1 | async-start | bytes 262144 | tf_op jit(solution)/shard_map/all_to_all | solution.py:236
  51.2 9.6 %all-to-all-done.1 = f32[3,64,16]{2,0,1:T(4,128)S(1)} async-done(((f32[3,64,16]{2,0,1:T(4,128)}), f32[3,64,16]{2,0,1:T(4,128)S(1)}, u32[]{:S(2)}, u32[]{:S(2)}) %all-to-all-start.1) | async-done | bytes 12320 | tf_op jit(solution)/shard_map/all_to_all | solution.py:236
  61.4 3.5 %collective-permute-start.12 = (f32[3,1,4,32]{3,2,1,0:T(4,128)S(1)}, f32[3,1,4,32]{3,2,1,0:T(4,128)S(1)}, u32[]{:S(2)}, u32[]{:S(2)}) collective-permute-start(f32[3,1,4,32]{3,2,1,0:T(4,128)S(1)} %get-tuple-element.115), channel_id=1, source_target_pairs={{0,64},{64,128},{128,192},{192,256},{256,320},{320,384},{384,448},... | collective-permute-start | bytes 4616 | tf_op jit(solution)/shard_map/ppermute | solution.py:22
  65.1 2.7 %collective-permute-start.10 = (bf16[20,20,2]{2,1,0:T(8,128)(2,1)S(1)}, bf16[20,20,2]{2,1,0:T(8,128)(2,1)S(1)}, u32[]{:S(2)}, u32[]{:S(2)}) collective-permute-start(bf16[20,20,2]{2,1,0:T(8,128)(2,1)S(1)} %get-tuple-element.90), channel_id=1, source_target_pairs={{0,1},{1,2},{2,3},{3,4},{4,5},{5,6},{6,7},{8,9},{9,10},{10,11},{11... | collective-permute-start | bytes 4808 | tf_op jit(solution)/shard_map/ppermute | solution.py:22
  71.6 3.6 %collective-permute-done.13 = f32[3,1,4,32]{3,2,1,0:T(4,128)S(1)} collective-permute-done((f32[3,1,4,32]{3,2,1,0:T(4,128)S(1)}, f32[3,1,4,32]{3,2,1,0:T(4,128)S(1)}, u32[]{:S(2)}, u32[]{:S(2)}) %collective-permute-start.13) | collective-permute-done | bytes 1568 | tf_op jit(solution)/shard_map/ppermute | solution.py:25
  75.3 2.6 %collective-permute-start.14 = (f32[3,6,1,32]{3,2,1,0:T(1,128)S(1)}, f32[3,6,1,32]{3,2,1,0:T(1,128)S(1)}, u32[]{:S(2)}, u32[]{:S(2)}) collective-permute-start(f32[3,6,1,32]{3,2,1,0:T(1,128)S(1)} %get-tuple-element.110), channel_id=1, source_target_pairs={{0,8},{8,16},{16,24},{24,32},{32,40},{40,48},{48,56},{1,9},{9,17},... | collective-permute-start | bytes 6920 | tf_op jit(solution)/shard_map/ppermute | solution.py:22
  83.0 5.6 %collective-permute-start.16 = (f32[3,6,6,1]{3,2,1,0:T(8,128)S(1)}, f32[3,6,6,1]{3,2,1,0:T(8,128)S(1)}, u32[]{:S(2)}, u32[]{:S(2)}) collective-permute-start(f32[3,6,6,1]{3,2,1,0:T(8,128)S(1)} %get-tuple-element.100), channel_id=1, source_target_pairs={{0,1},{1,2},{2,3},{3,4},{4,5},{5,6},{6,7},{8,9},{9,10},{10,11},{11... | collective-permute-start | bytes 1304 | tf_op jit(solution)/shard_map/ppermute | solution.py:22
  90.9 3.3 %collective-permute-done.17 = f32[3,6,6,1]{3,2,1,0:T(8,128)S(1)} collective-permute-done((f32[3,6,6,1]{3,2,1,0:T(8,128)S(1)}, f32[3,6,6,1]{3,2,1,0:T(8,128)S(1)}, u32[]{:S(2)}, u32[]{:S(2)}) %collective-permute-start.17) | collective-permute-done | bytes 464 | tf_op jit(solution)/shard_map/ppermute | solution.py:25
  97.3 3.8 %collective-permute-start.2 = (bf16[2,26,5,128]{3,2,1,0:T(8,128)(2,1)S(1)}, bf16[2,26,5,128]{3,2,1,0:T(8,128)(2,1)S(1)}, u32[]{:S(2)}, u32[]{:S(2)}) collective-permute-start(bf16[2,26,5,128]{3,2,1,0:T(8,128)(2,1)S(1)} %get-tuple-element.78), channel_id=1, source_target_pairs={{0,8},{8,16},{16,24},{24,32},{32,40},{40,48},{48,56},{1,9},{9,17},... | collective-permute-start | bytes 199688 | tf_op jit(solution)/shard_map/ppermute | solution.py:22
  102.8 3.8 %collective-permute-done.3 = bf16[2,26,5,128]{3,2,1,0:T(8,128)(2,1)S(1)} collective-permute-done((bf16[2,26,5,128]{3,2,1,0:T(8,128)(2,1)S(1)}, bf16[2,26,5,128]{3,2,1,0:T(8,128)(2,1)S(1)}, u32[]{:S(2)}, u32[]{:S(2)}) %collective-permute-start.3) | collective-permute-done | bytes 66592 | tf_op jit(solution)/shard_map/ppermute | solution.py:25
  107.8 4.1 %collective-permute-start.4 = (bf16[2,26,26,5]{3,2,1,0:T(8,128)(2,1)}, bf16[2,26,26,5]{3,2,1,0:T(8,128)(2,1)}, u32[]{:S(2)}, u32[]{:S(2)}) collective-permute-start(bf16[2,26,26,5]{3,2,1,0:T(8,128)(2,1)} %get-tuple-element.64), channel_id=1, source_target_pairs={{0,1},{1,2},{2,3},{3,4},{4,5},{5,6},{6,7},{8,9},{9,10},{10,11},{11... | collective-permute-start | bytes 40568 | tf_op jit(solution)/shard_map/ppermute | solution.py:22
  117.4 4.4 %collective-permute-done.5 = bf16[2,26,26,5]{3,2,1,0:T(8,128)(2,1)} collective-permute-done((bf16[2,26,26,5]{3,2,1,0:T(8,128)(2,1)}, bf16[2,26,26,5]{3,2,1,0:T(8,128)(2,1)}, u32[]{:S(2)}, u32[]{:S(2)}) %collective-permute-start.5) | collective-permute-done | bytes 13552 | tf_op jit(solution)/shard_map/ppermute | solution.py:25
  133.4 18.6 %all_to_all.46 = f32[6,64,16]{2,0,1:T(8,128)S(1)} all-to-all(f32[6,64,16]{2,0,1:T(8,128)S(1)} %copy.121), channel_id=1, replica_groups=mesh['gx'=8,'gy'=8,'gz'=8] {'gy','gz'}, dimensions={1} | all-to-all | bytes 49152 | tf_op jit(solution)/shard_map/all_to_all | solution.py:263
  153.1 15.6 %all_to_all.47 = f32[3,64,16]{2,0,1:T(4,128)S(1)} all-to-all(f32[3,64,16]{2,0,1:T(4,128)S(1)} %copy.125), channel_id=1, replica_groups=mesh['gx'=8,'gy'=8,'gz'=8] {'gy','gz'}, dimensions={1} | all-to-all | bytes 24576 | tf_op jit(solution)/shard_map/all_to_all | solution.py:236
  169.4 5.1 %collective-permute-start.18 = (f32[3,1,4,32]{3,2,1,0:T(4,128)S(1)}, f32[3,1,4,32]{3,2,1,0:T(4,128)S(1)}, u32[]{:S(2)}, u32[]{:S(2)}) collective-permute-start(f32[3,1,4,32]{3,2,1,0:T(4,128)S(1)} %get-tuple-element.113), channel_id=1, source_target_pairs={{0,64},{64,128},{128,192},{192,256},{256,320},{320,384},{384,448},... | collective-permute-start | bytes 4616 | tf_op jit(solution)/shard_map/ppermute | solution.py:22
  176.5 3.6 %collective-permute-done.19 = f32[3,1,4,32]{3,2,1,0:T(4,128)S(1)} collective-permute-done((f32[3,1,4,32]{3,2,1,0:T(4,128)S(1)}, f32[3,1,4,32]{3,2,1,0:T(4,128)S(1)}, u32[]{:S(2)}, u32[]{:S(2)}) %collective-permute-start.19) | collective-permute-done | bytes 1568 | tf_op jit(solution)/shard_map/ppermute | solution.py:25
  183.7 3.1 %collective-permute-done.21 = f32[3,6,1,32]{3,2,1,0:T(1,128)S(1)} collective-permute-done((f32[3,6,1,32]{3,2,1,0:T(1,128)S(1)}, f32[3,6,1,32]{3,2,1,0:T(1,128)S(1)}, u32[]{:S(2)}, u32[]{:S(2)}) %collective-permute-start.21) | collective-permute-done | bytes 2336 | tf_op jit(solution)/shard_map/ppermute | solution.py:25
  187.0 5.5 %collective-permute-start.22 = (f32[3,6,6,1]{3,2,1,0:T(8,128)S(1)}, f32[3,6,6,1]{3,2,1,0:T(8,128)S(1)}, u32[]{:S(2)}, u32[]{:S(2)}) collective-permute-start(f32[3,6,6,1]{3,2,1,0:T(8,128)S(1)} %get-tuple-element.96), channel_id=1, source_target_pairs={{0,1},{1,2},{2,3},{3,4},{4,5},{5,6},{6,7},{8,9},{9,10},{10,11},{11... | collective-permute-start | bytes 1304 | tf_op jit(solution)/shard_map/ppermute | solution.py:22
  194.4 3.7 %collective-permute-done.23 = f32[3,6,6,1]{3,2,1,0:T(8,128)S(1)} collective-permute-done((f32[3,6,6,1]{3,2,1,0:T(8,128)S(1)}, f32[3,6,6,1]{3,2,1,0:T(8,128)S(1)}, u32[]{:S(2)}, u32[]{:S(2)}) %collective-permute-start.23) | collective-permute-done | bytes 464 | tf_op jit(solution)/shard_map/ppermute | solution.py:25
  205.2 18.3 %all_to_all.48 = f32[6,64,16]{2,0,1:T(8,128)S(1)} all-to-all(f32[6,64,16]{2,0,1:T(8,128)S(1)} %copy.133), channel_id=1, replica_groups=mesh['gx'=8,'gy'=8,'gz'=8] {'gy','gz'}, dimensions={1} | all-to-all | bytes 49152 | tf_op jit(solution)/shard_map/all_to_all | solution.py:263
  (342 shorter events, 65.2 us)
Async XLA Ops:
  3.1 32.1 %all-to-all-start = ((f32[1,64,2]{2,0,1:T(1,128)}), f32[1,64,2]{2,0,1:T(1,128)S(1)}, u32[]{:S(2)}, u32[]{:S(2)}) async-start(f32[1,64,2]{2,0,1:T(1,128)} %bitcast.2), calls=%async_computation | async-start | bytes 65536 | tf_op jit(solution)/shard_map/all_to_all | solution.py:239
  14.7 82.5 %collective-permute-start = (bf16[2,5,16,128]{3,2,1,0:T(8,128)(2,1)S(1)}, bf16[2,5,16,128]{3,2,1,0:T(8,128)(2,1)S(1)}, u32[]{:S(2)}, u32[]{:S(2)}) collective-permute-start(bf16[2,5,16,128]{3,2,1,0:T(8,128)(2,1)S(1)} %get-tuple-element.88), channel_id=1, source_target_pairs={{0,64},{64,128},{128,192},{192,256},{256,320},{320,384},{384,448},... | collective-permute-start | bytes 122888 | tf_op jit(solution)/shard_map/ppermute | solution.py:22
  20.9 8.7 %collective-permute-start.6 = (bf16[2,16,128]{2,1,0:T(8,128)(2,1)S(1)}, bf16[2,16,128]{2,1,0:T(8,128)(2,1)S(1)}, u32[]{:S(2)}, u32[]{:S(2)}) collective-permute-start(bf16[2,16,128]{2,1,0:T(8,128)(2,1)S(1)} %get-tuple-element.102), channel_id=1, source_target_pairs={{0,64},{64,128},{128,192},{192,256},{256,320},{320,384},{384,448},... | collective-permute-start | bytes 24584 | tf_op jit(solution)/shard_map/ppermute | solution.py:22
  24.0 5.6 %collective-permute-start.7 = (bf16[2,16,128]{2,1,0:T(8,128)(2,1)S(1)}, bf16[2,16,128]{2,1,0:T(8,128)(2,1)S(1)}, u32[]{:S(2)}, u32[]{:S(2)}) collective-permute-start(bf16[2,16,128]{2,1,0:T(8,128)(2,1)S(1)} %get-tuple-element.103), channel_id=1, source_target_pairs={{64,0},{128,64},{192,128},{256,192},{320,256},{384,320},{448,384},... | collective-permute-start | bytes 24584 | tf_op jit(solution)/shard_map/ppermute | solution.py:25
  29.7 21.5 %collective-permute-start.8 = (bf16[20,2,128]{2,1,0:T(2,128)(2,1)S(1)}, bf16[20,2,128]{2,1,0:T(2,128)(2,1)S(1)}, u32[]{:S(2)}, u32[]{:S(2)}) collective-permute-start(bf16[20,2,128]{2,1,0:T(2,128)(2,1)S(1)} %get-tuple-element.92), channel_id=1, source_target_pairs={{0,8},{8,16},{16,24},{24,32},{32,40},{40,48},{48,56},{1,9},{9,17},... | collective-permute-start | bytes 30728 | tf_op jit(solution)/shard_map/ppermute | solution.py:22
  33.0 18.2 %collective-permute-start.9 = (bf16[20,2,128]{2,1,0:T(2,128)(2,1)S(1)}, bf16[20,2,128]{2,1,0:T(2,128)(2,1)S(1)}, u32[]{:S(2)}, u32[]{:S(2)}) collective-permute-start(bf16[20,2,128]{2,1,0:T(2,128)(2,1)S(1)} %get-tuple-element.93), channel_id=1, source_target_pairs={{8,0},{16,8},{24,16},{32,24},{40,32},{48,40},{56,48},{9,1},{17,9},... | collective-permute-start | bytes 30728 | tf_op jit(solution)/shard_map/ppermute | solution.py:25
  35.2 25.5 %all-to-all-start.1 = ((f32[3,64,16]{2,0,1:T(4,128)}), f32[3,64,16]{2,0,1:T(4,128)S(1)}, u32[]{:S(2)}, u32[]{:S(2)}) async-start(f32[3,64,16]{2,0,1:T(4,128)} %copy.112), calls=%async_computation.1 | async-start | bytes 262144 | tf_op jit(solution)/shard_map/all_to_all | solution.py:236
  61.4 10.2 %collective-permute-start.12 = (f32[3,1,4,32]{3,2,1,0:T(4,128)S(1)}, f32[3,1,4,32]{3,2,1,0:T(4,128)S(1)}, u32[]{:S(2)}, u32[]{:S(2)}) collective-permute-start(f32[3,1,4,32]{3,2,1,0:T(4,128)S(1)} %get-tuple-element.115), channel_id=1, source_target_pairs={{0,64},{64,128},{128,192},{192,256},{256,320},{320,384},{384,448},... | collective-permute-start | bytes 4616 | tf_op jit(solution)/shard_map/ppermute | solution.py:22
  65.1 14.8 %collective-permute-start.10 = (bf16[20,20,2]{2,1,0:T(8,128)(2,1)S(1)}, bf16[20,20,2]{2,1,0:T(8,128)(2,1)S(1)}, u32[]{:S(2)}, u32[]{:S(2)}) collective-permute-start(bf16[20,20,2]{2,1,0:T(8,128)(2,1)S(1)} %get-tuple-element.90), channel_id=1, source_target_pairs={{0,1},{1,2},{2,3},{3,4},{4,5},{5,6},{6,7},{8,9},{9,10},{10,11},{11... | collective-permute-start | bytes 4808 | tf_op jit(solution)/shard_map/ppermute | solution.py:22
  67.7 14.6 %collective-permute-start.11 = (bf16[20,20,2]{2,1,0:T(8,128)(2,1)S(1)}, bf16[20,20,2]{2,1,0:T(8,128)(2,1)S(1)}, u32[]{:S(2)}, u32[]{:S(2)}) collective-permute-start(bf16[20,20,2]{2,1,0:T(8,128)(2,1)S(1)} %get-tuple-element.91), channel_id=1, source_target_pairs={{1,0},{2,1},{3,2},{4,3},{5,4},{6,5},{7,6},{9,8},{10,9},{11,10},{12... | collective-permute-start | bytes 4808 | tf_op jit(solution)/shard_map/ppermute | solution.py:25
  69.7 5.6 %collective-permute-start.13 = (f32[3,1,4,32]{3,2,1,0:T(4,128)S(1)}, f32[3,1,4,32]{3,2,1,0:T(4,128)S(1)}, u32[]{:S(2)}, u32[]{:S(2)}) collective-permute-start(f32[3,1,4,32]{3,2,1,0:T(4,128)S(1)} %get-tuple-element.114), channel_id=1, source_target_pairs={{64,0},{128,64},{192,128},{256,192},{320,256},{384,320},{448,384},... | collective-permute-start | bytes 4616 | tf_op jit(solution)/shard_map/ppermute | solution.py:25
  75.3 7.6 %collective-permute-start.14 = (f32[3,6,1,32]{3,2,1,0:T(1,128)S(1)}, f32[3,6,1,32]{3,2,1,0:T(1,128)S(1)}, u32[]{:S(2)}, u32[]{:S(2)}) collective-permute-start(f32[3,6,1,32]{3,2,1,0:T(1,128)S(1)} %get-tuple-element.110), channel_id=1, source_target_pairs={{0,8},{8,16},{16,24},{24,32},{32,40},{40,48},{48,56},{1,9},{9,17},... | collective-permute-start | bytes 6920 | tf_op jit(solution)/shard_map/ppermute | solution.py:22
  77.8 5.0 %collective-permute-start.15 = (f32[3,6,1,32]{3,2,1,0:T(1,128)S(1)}, f32[3,6,1,32]{3,2,1,0:T(1,128)S(1)}, u32[]{:S(2)}, u32[]{:S(2)}) collective-permute-start(f32[3,6,1,32]{3,2,1,0:T(1,128)S(1)} %get-tuple-element.111), channel_id=1, source_target_pairs={{8,0},{16,8},{24,16},{32,24},{40,32},{48,40},{56,48},{9,1},{17,9},... | collective-permute-start | bytes 6920 | tf_op jit(solution)/shard_map/ppermute | solution.py:25
  79.9 17.3 %collective-permute-start.1 = (bf16[2,5,16,128]{3,2,1,0:T(8,128)(2,1)S(1)}, bf16[2,5,16,128]{3,2,1,0:T(8,128)(2,1)S(1)}, u32[]{:S(2)}, u32[]{:S(2)}) collective-permute-start(bf16[2,5,16,128]{3,2,1,0:T(8,128)(2,1)S(1)} %get-tuple-element.89), channel_id=1, source_target_pairs={{64,0},{128,64},{192,128},{256,192},{320,256},{384,320},{448,384},... | collective-permute-start | bytes 122888 | tf_op jit(solution)/shard_map/ppermute | solution.py:25
  83.0 7.9 %collective-permute-start.16 = (f32[3,6,6,1]{3,2,1,0:T(8,128)S(1)}, f32[3,6,6,1]{3,2,1,0:T(8,128)S(1)}, u32[]{:S(2)}, u32[]{:S(2)}) collective-permute-start(f32[3,6,6,1]{3,2,1,0:T(8,128)S(1)} %get-tuple-element.100), channel_id=1, source_target_pairs={{0,1},{1,2},{2,3},{3,4},{4,5},{5,6},{6,7},{8,9},{9,10},{10,11},{11... | collective-permute-start | bytes 1304 | tf_op jit(solution)/shard_map/ppermute | solution.py:22
  88.6 5.7 %collective-permute-start.17 = (f32[3,6,6,1]{3,2,1,0:T(8,128)S(1)}, f32[3,6,6,1]{3,2,1,0:T(8,128)S(1)}, u32[]{:S(2)}, u32[]{:S(2)}) collective-permute-start(f32[3,6,6,1]{3,2,1,0:T(8,128)S(1)} %get-tuple-element.101), channel_id=1, source_target_pairs={{1,0},{2,1},{3,2},{4,3},{5,4},{6,5},{7,6},{9,8},{10,9},{11,10},{12... | collective-permute-start | bytes 1304 | tf_op jit(solution)/shard_map/ppermute | solution.py:25
  97.3 5.5 %collective-permute-start.2 = (bf16[2,26,5,128]{3,2,1,0:T(8,128)(2,1)S(1)}, bf16[2,26,5,128]{3,2,1,0:T(8,128)(2,1)S(1)}, u32[]{:S(2)}, u32[]{:S(2)}) collective-permute-start(bf16[2,26,5,128]{3,2,1,0:T(8,128)(2,1)S(1)} %get-tuple-element.78), channel_id=1, source_target_pairs={{0,8},{8,16},{16,24},{24,32},{32,40},{40,48},{48,56},{1,9},{9,17},... | collective-permute-start | bytes 199688 | tf_op jit(solution)/shard_map/ppermute | solution.py:22
  101.1 5.4 %collective-permute-start.3 = (bf16[2,26,5,128]{3,2,1,0:T(8,128)(2,1)S(1)}, bf16[2,26,5,128]{3,2,1,0:T(8,128)(2,1)S(1)}, u32[]{:S(2)}, u32[]{:S(2)}) collective-permute-start(bf16[2,26,5,128]{3,2,1,0:T(8,128)(2,1)S(1)} %get-tuple-element.79), channel_id=1, source_target_pairs={{8,0},{16,8},{24,16},{32,24},{40,32},{48,40},{56,48},{9,1},{17,9},... | collective-permute-start | bytes 199688 | tf_op jit(solution)/shard_map/ppermute | solution.py:25
  107.8 9.5 %collective-permute-start.4 = (bf16[2,26,26,5]{3,2,1,0:T(8,128)(2,1)}, bf16[2,26,26,5]{3,2,1,0:T(8,128)(2,1)}, u32[]{:S(2)}, u32[]{:S(2)}) collective-permute-start(bf16[2,26,26,5]{3,2,1,0:T(8,128)(2,1)} %get-tuple-element.64), channel_id=1, source_target_pairs={{0,1},{1,2},{2,3},{3,4},{4,5},{5,6},{6,7},{8,9},{9,10},{10,11},{11... | collective-permute-start | bytes 40568 | tf_op jit(solution)/shard_map/ppermute | solution.py:22
  112.0 9.8 %collective-permute-start.5 = (bf16[2,26,26,5]{3,2,1,0:T(8,128)(2,1)}, bf16[2,26,26,5]{3,2,1,0:T(8,128)(2,1)}, u32[]{:S(2)}, u32[]{:S(2)}) collective-permute-start(bf16[2,26,26,5]{3,2,1,0:T(8,128)(2,1)} %get-tuple-element.65), channel_id=1, source_target_pairs={{1,0},{2,1},{3,2},{4,3},{5,4},{6,5},{7,6},{9,8},{10,9},{11,10},{12... | collective-permute-start | bytes 40568 | tf_op jit(solution)/shard_map/ppermute | solution.py:25
  169.4 7.0 %collective-permute-start.18 = (f32[3,1,4,32]{3,2,1,0:T(4,128)S(1)}, f32[3,1,4,32]{3,2,1,0:T(4,128)S(1)}, u32[]{:S(2)}, u32[]{:S(2)}) collective-permute-start(f32[3,1,4,32]{3,2,1,0:T(4,128)S(1)} %get-tuple-element.113), channel_id=1, source_target_pairs={{0,64},{64,128},{128,192},{192,256},{256,320},{320,384},{384,448},... | collective-permute-start | bytes 4616 | tf_op jit(solution)/shard_map/ppermute | solution.py:22
  174.5 5.6 %collective-permute-start.19 = (f32[3,1,4,32]{3,2,1,0:T(4,128)S(1)}, f32[3,1,4,32]{3,2,1,0:T(4,128)S(1)}, u32[]{:S(2)}, u32[]{:S(2)}) collective-permute-start(f32[3,1,4,32]{3,2,1,0:T(4,128)S(1)} %get-tuple-element.112), channel_id=1, source_target_pairs={{64,0},{128,64},{192,128},{256,192},{320,256},{384,320},{448,384},... | collective-permute-start | bytes 4616 | tf_op jit(solution)/shard_map/ppermute | solution.py:25
  187.0 7.4 %collective-permute-start.22 = (f32[3,6,6,1]{3,2,1,0:T(8,128)S(1)}, f32[3,6,6,1]{3,2,1,0:T(8,128)S(1)}, u32[]{:S(2)}, u32[]{:S(2)}) collective-permute-start(f32[3,6,6,1]{3,2,1,0:T(8,128)S(1)} %get-tuple-element.96), channel_id=1, source_target_pairs={{0,1},{1,2},{2,3},{3,4},{4,5},{5,6},{6,7},{8,9},{9,10},{10,11},{11... | collective-permute-start | bytes 1304 | tf_op jit(solution)/shard_map/ppermute | solution.py:22
  192.4 5.7 %collective-permute-start.23 = (f32[3,6,6,1]{3,2,1,0:T(8,128)S(1)}, f32[3,6,6,1]{3,2,1,0:T(8,128)S(1)}, u32[]{:S(2)}, u32[]{:S(2)}) collective-permute-start(f32[3,6,6,1]{3,2,1,0:T(8,128)S(1)} %get-tuple-element.97), channel_id=1, source_target_pairs={{1,0},{2,1},{3,2},{4,3},{5,4},{6,5},{7,6},{9,8},{10,9},{11,10},{12... | collective-permute-start | bytes 1304 | tf_op jit(solution)/shard_map/ppermute | solution.py:25
  (49 other events, 855.9 us)
where the time goes:
time: 226 us; the launch traced here: 225 us
  starting transfers between devices  92.9 us (41%)
  blocking collectives  52.5 us (23%)
  waiting for transfers between devices  37.7 us (17%)
  other arithmetic  20.4 us (9%)
  local copies, waits for them, and re-layouts  11 us (5%)
  matrix products  8 us (4%)
    ppermute x12, starting transfers between devices, with_halo(): lax.ppermute(lax.slice_in_dim(block, block.shape[dim] - width, None, axis...  46.7 us
    all_to_all x2, blocking collectives, per_device(): lax.all_to_all(outgoing, ('gy', 'gz'), split_axis=1, concat_axis=1, tiled...  36.9 us
    ppermute x12, waiting for transfers between devices, with_halo(): lax.ppermute(lax.slice_in_dim(block, 0, width, axis=dim), axis, backward)  25.6 us
    ppermute x12, starting transfers between devices, with_halo(): lax.ppermute(lax.slice_in_dim(block, 0, width, axis=dim), axis, backward)  21 us
    all_to_all x1, blocking collectives, per_device(): lax.all_to_all(send_outgoing, ('gy', 'gz'), split_axis=1, concat_axis=1,...  15.6 us
    all_to_all x1, starting transfers between devices, per_device(): lax.all_to_all(send_outgoing, ('gy', 'gz'), split_axis=1, concat_axis=1,...  14.4 us
    all_to_all x1, starting transfers between devices, per_device(): lax.all_to_all(labels, ('gy', 'gz'), split_axis=1, concat_axis=1, tiled=T...  10.8 us
    all_to_all x1, waiting for transfers between devices, per_device(): lax.all_to_all(send_outgoing, ('gy', 'gz'), split_axis=1, concat_axis=1,...  9.59 us
  transfers between devices with their start and end apart: 26, of which 10 were waited for; matrix products, arithmetic and copies ran while one was open for 6% of the time, Pallas kernels for 0%

commit v1 on v0

--- a/solution.py
+++ b/solution.py
@@ -260,7 +260,15 @@
         outgoing = jnp.einsum("ckn,pk->cpn", sums, send_placing, precision=highest).reshape(
             channels, -1
         )
-        incoming = lax.all_to_all(outgoing, ("gy", "gz"), split_axis=1, concat_axis=1, tiled=True)
+        incoming = jnp.concatenate(
+            jax.lax.all_to_all(
+                jnp.stack(jnp.split(outgoing, jax.lax.axis_size(("gy", "gz")), axis=1), axis=0),
+                ("gy", "gz"),
+                0,
+                0,
+            ),
+            axis=1,
+        )
         returned = jnp.einsum(
             "cpn,jp->cjn", incoming.reshape(channels, members * CAP, -1), packing, precision=highest
         )

time: 226 us -> 234 us (1.035)
  local copies, waits for them, and re-layouts: 11 us -> 19 us
    unnamed x98 -> x224, local copies, waits for them, and re-layouts: 0.59 us -> 8.49 us
where the time goes in v1:
time: 234 us; the launch traced here: 232 us
  starting transfers between devices  92.6 us (40%)
  blocking collectives  52.5 us (22%)
  waiting for transfers between devices  37.7 us (16%)
  other arithmetic  20.4 us (9%)
  local copies, waits for them, and re-layouts  19 us (8%)
  matrix products  8 us (3%)
    ppermute x12, starting transfers between devices, with_halo(): lax.ppermute(lax.slice_in_dim(block, block.shape[dim] - width, None, axis...  46.4 us
    all_to_all x2, blocking collectives, per_device(): jax.lax.all_to_all(jnp.stack(jnp.split(outgoing, jax.lax.axis_size(('gy',...  36.9 us
    ppermute x12, waiting for transfers between devices, with_halo(): lax.ppermute(lax.slice_in_dim(block, 0, width, axis=dim), axis, backward)  25.6 us
    ppermute x12, starting transfers between devices, with_halo(): lax.ppermute(lax.slice_in_dim(block, 0, width, axis=dim), axis, backward)  21 us
    all_to_all x1, blocking collectives, per_device(): lax.all_to_all(send_outgoing, ('gy', 'gz'), split_axis=1, concat_axis=1,...  15.6 us
    all_to_all x1, starting transfers between devices, per_device(): lax.all_to_all(send_outgoing, ('gy', 'gz'), split_axis=1, concat_axis=1,...  14.4 us
    all_to_all x1, starting transfers between devices, per_device(): lax.all_to_all(labels, ('gy', 'gz'), split_axis=1, concat_axis=1, tiled=T...  10.8 us
    all_to_all x1, waiting for transfers between devices, per_device(): lax.all_to_all(send_outgoing, ('gy', 'gz'), split_axis=1, concat_axis=1,...  9.59 us
  transfers between devices with their start and end apart: 26, of which 10 were waited for; matrix products, arithmetic and copies ran while one was open for 6% of the time, Pallas kernels for 0%

profile of v1, /device:TPU:193, one launch (start us, length us, event | category | flops | bytes accessed | tf_op | source)
XLA Modules:
  0.0 232.5 jit_solution(16767217807629804257)
XLA Ops:
  3.1 10.8 %all-to-all-start = ((f32[1,64,2]{2,0,1:T(1,128)}), f32[1,64,2]{2,0,1:T(1,128)S(1)}, u32[]{:S(2)}, u32[]{:S(2)}) async-start(f32[1,64,2]{2,0,1:T(1,128)} %bitcast.2), calls=%async_computation | async-start | bytes 65536 | tf_op jit(solution)/shard_map/all_to_all | solution.py:239
  14.7 5.2 %collective-permute-start = (bf16[2,5,16,128]{3,2,1,0:T(8,128)(2,1)S(1)}, bf16[2,5,16,128]{3,2,1,0:T(8,128)(2,1)S(1)}, u32[]{:S(2)}, u32[]{:S(2)}) collective-permute-start(bf16[2,5,16,128]{3,2,1,0:T(8,128)(2,1)S(1)} %get-tuple-element.88), channel_id=1, source_target_pairs={{0,64},{64,128},{128,192},{192,256},{256,320},{320,384},{384,448},... | collective-permute-start | bytes 122888 | tf_op jit(solution)/shard_map/ppermute | solution.py:22
  20.9 3.1 %collective-permute-start.6 = (bf16[2,16,128]{2,1,0:T(8,128)(2,1)S(1)}, bf16[2,16,128]{2,1,0:T(8,128)(2,1)S(1)}, u32[]{:S(2)}, u32[]{:S(2)}) collective-permute-start(bf16[2,16,128]{2,1,0:T(8,128)(2,1)S(1)} %get-tuple-element.102), channel_id=1, source_target_pairs={{0,64},{64,128},{128,192},{192,256},{256,320},{320,384},{384,448},... | collective-permute-start | bytes 24584 | tf_op jit(solution)/shard_map/ppermute | solution.py:22
  29.7 3.3 %collective-permute-start.8 = (bf16[20,2,128]{2,1,0:T(2,128)(2,1)S(1)}, bf16[20,2,128]{2,1,0:T(2,128)(2,1)S(1)}, u32[]{:S(2)}, u32[]{:S(2)}) collective-permute-start(bf16[20,2,128]{2,1,0:T(2,128)(2,1)S(1)} %get-tuple-element.92), channel_id=1, source_target_pairs={{0,8},{8,16},{16,24},{24,32},{32,40},{40,48},{48,56},{1,9},{9,17},... | collective-permute-start | bytes 30728 | tf_op jit(solution)/shard_map/ppermute | solution.py:22
  35.2 14.4 %all-to-all-start.1 = ((f32[3,64,16]{2,0,1:T(4,128)}), f32[3,64,16]{2,0,1:T(4,128)S(1)}, u32[]{:S(2)}, u32[]{:S(2)}) async-start(f32[3,64,16]{2,0,1:T(4,128)} %copy.528), calls=%async_computation.1 | async-start | bytes 262144 | tf_op jit(solution)/shard_map/all_to_all | solution.py:236
  51.2 9.6 %all-to-all-done.1 = f32[3,64,16]{2,0,1:T(4,128)S(1)} async-done(((f32[3,64,16]{2,0,1:T(4,128)}), f32[3,64,16]{2,0,1:T(4,128)S(1)}, u32[]{:S(2)}, u32[]{:S(2)}) %all-to-all-start.1) | async-done | bytes 12320 | tf_op jit(solution)/shard_map/all_to_all | solution.py:236
  61.4 3.5 %collective-permute-start.12 = (f32[3,1,4,32]{3,2,1,0:T(4,128)S(1)}, f32[3,1,4,32]{3,2,1,0:T(4,128)S(1)}, u32[]{:S(2)}, u32[]{:S(2)}) collective-permute-start(f32[3,1,4,32]{3,2,1,0:T(4,128)S(1)} %get-tuple-element.115), channel_id=1, source_target_pairs={{0,64},{64,128},{128,192},{192,256},{256,320},{320,384},{384,448},... | collective-permute-start | bytes 4616 | tf_op jit(solution)/shard_map/ppermute | solution.py:22
  65.1 2.7 %collective-permute-start.10 = (bf16[20,20,2]{2,1,0:T(8,128)(2,1)S(1)}, bf16[20,20,2]{2,1,0:T(8,128)(2,1)S(1)}, u32[]{:S(2)}, u32[]{:S(2)}) collective-permute-start(bf16[20,20,2]{2,1,0:T(8,128)(2,1)S(1)} %get-tuple-element.90), channel_id=1, source_target_pairs={{0,1},{1,2},{2,3},{3,4},{4,5},{5,6},{6,7},{8,9},{9,10},{10,11},{11... | collective-permute-start | bytes 4808 | tf_op jit(solution)/shard_map/ppermute | solution.py:22
  71.6 3.6 %collective-permute-done.13 = f32[3,1,4,32]{3,2,1,0:T(4,128)S(1)} collective-permute-done((f32[3,1,4,32]{3,2,1,0:T(4,128)S(1)}, f32[3,1,4,32]{3,2,1,0:T(4,128)S(1)}, u32[]{:S(2)}, u32[]{:S(2)}) %collective-permute-start.13) | collective-permute-done | bytes 1568 | tf_op jit(solution)/shard_map/ppermute | solution.py:25
  75.3 2.6 %collective-permute-start.14 = (f32[3,6,1,32]{3,2,1,0:T(1,128)S(1)}, f32[3,6,1,32]{3,2,1,0:T(1,128)S(1)}, u32[]{:S(2)}, u32[]{:S(2)}) collective-permute-start(f32[3,6,1,32]{3,2,1,0:T(1,128)S(1)} %get-tuple-element.110), channel_id=1, source_target_pairs={{0,8},{8,16},{16,24},{24,32},{32,40},{40,48},{48,56},{1,9},{9,17},... | collective-permute-start | bytes 6920 | tf_op jit(solution)/shard_map/ppermute | solution.py:22
  83.0 5.6 %collective-permute-start.16 = (f32[3,6,6,1]{3,2,1,0:T(8,128)S(1)}, f32[3,6,6,1]{3,2,1,0:T(8,128)S(1)}, u32[]{:S(2)}, u32[]{:S(2)}) collective-permute-start(f32[3,6,6,1]{3,2,1,0:T(8,128)S(1)} %get-tuple-element.100), channel_id=1, source_target_pairs={{0,1},{1,2},{2,3},{3,4},{4,5},{5,6},{6,7},{8,9},{9,10},{10,11},{11... | collective-permute-start | bytes 1304 | tf_op jit(solution)/shard_map/ppermute | solution.py:22
  90.9 3.3 %collective-permute-done.17 = f32[3,6,6,1]{3,2,1,0:T(8,128)S(1)} collective-permute-done((f32[3,6,6,1]{3,2,1,0:T(8,128)S(1)}, f32[3,6,6,1]{3,2,1,0:T(8,128)S(1)}, u32[]{:S(2)}, u32[]{:S(2)}) %collective-permute-start.17) | collective-permute-done | bytes 464 | tf_op jit(solution)/shard_map/ppermute | solution.py:25
  97.3 3.8 %collective-permute-start.2 = (bf16[2,26,5,128]{3,2,1,0:T(8,128)(2,1)S(1)}, bf16[2,26,5,128]{3,2,1,0:T(8,128)(2,1)S(1)}, u32[]{:S(2)}, u32[]{:S(2)}) collective-permute-start(bf16[2,26,5,128]{3,2,1,0:T(8,128)(2,1)S(1)} %get-tuple-element.78), channel_id=1, source_target_pairs={{0,8},{8,16},{16,24},{24,32},{32,40},{40,48},{48,56},{1,9},{9,17},... | collective-permute-start | bytes 199688 | tf_op jit(solution)/shard_map/ppermute | solution.py:22
  102.8 3.8 %collective-permute-done.3 = bf16[2,26,5,128]{3,2,1,0:T(8,128)(2,1)S(1)} collective-permute-done((bf16[2,26,5,128]{3,2,1,0:T(8,128)(2,1)S(1)}, bf16[2,26,5,128]{3,2,1,0:T(8,128)(2,1)S(1)}, u32[]{:S(2)}, u32[]{:S(2)}) %collective-permute-start.3) | collective-permute-done | bytes 66592 | tf_op jit(solution)/shard_map/ppermute | solution.py:25
  107.8 4.1 %collective-permute-start.4 = (bf16[2,26,26,5]{3,2,1,0:T(8,128)(2,1)}, bf16[2,26,26,5]{3,2,1,0:T(8,128)(2,1)}, u32[]{:S(2)}, u32[]{:S(2)}) collective-permute-start(bf16[2,26,26,5]{3,2,1,0:T(8,128)(2,1)} %get-tuple-element.64), channel_id=1, source_target_pairs={{0,1},{1,2},{2,3},{3,4},{4,5},{5,6},{6,7},{8,9},{9,10},{10,11},{11... | collective-permute-start | bytes 40568 | tf_op jit(solution)/shard_map/ppermute | solution.py:22
  117.4 4.4 %collective-permute-done.5 = bf16[2,26,26,5]{3,2,1,0:T(8,128)(2,1)} collective-permute-done((bf16[2,26,26,5]{3,2,1,0:T(8,128)(2,1)}, bf16[2,26,26,5]{3,2,1,0:T(8,128)(2,1)}, u32[]{:S(2)}, u32[]{:S(2)}) %collective-permute-start.5) | collective-permute-done | bytes 13552 | tf_op jit(solution)/shard_map/ppermute | solution.py:25
  137.4 18.6 %all_to_all.38 = f32[64,6,16]{2,1,0:T(8,128)S(1)} all-to-all(f32[64,6,16]{2,1,0:T(8,128)S(1)} %constant_dynamic-update-slice_fusion.3), channel_id=1, replica_groups=mesh['gx'=8,'gy'=8,'gz'=8] {'gy','gz'}, dimensions={0} | all-to-all | bytes 49152 | tf_op jit(solution)/shard_map/all_to_all | solution.py:264
  157.1 15.6 %all_to_all.39 = f32[3,64,16]{2,0,1:T(4,128)S(1)} all-to-all(f32[3,64,16]{2,0,1:T(4,128)S(1)} %copy.540), channel_id=1, replica_groups=mesh['gx'=8,'gy'=8,'gz'=8] {'gy','gz'}, dimensions={1} | all-to-all | bytes 24576 | tf_op jit(solution)/shard_map/all_to_all | solution.py:236
  173.4 4.9 %collective-permute-start.18 = (f32[3,1,4,32]{3,2,1,0:T(4,128)S(1)}, f32[3,1,4,32]{3,2,1,0:T(4,128)S(1)}, u32[]{:S(2)}, u32[]{:S(2)}) collective-permute-start(f32[3,1,4,32]{3,2,1,0:T(4,128)S(1)} %get-tuple-element.113), channel_id=1, source_target_pairs={{0,64},{64,128},{128,192},{192,256},{256,320},{320,384},{384,448},... | collective-permute-start | bytes 4616 | tf_op jit(solution)/shard_map/ppermute | solution.py:22
  180.3 3.6 %collective-permute-done.19 = f32[3,1,4,32]{3,2,1,0:T(4,128)S(1)} collective-permute-done((f32[3,1,4,32]{3,2,1,0:T(4,128)S(1)}, f32[3,1,4,32]{3,2,1,0:T(4,128)S(1)}, u32[]{:S(2)}, u32[]{:S(2)}) %collective-permute-start.19) | collective-permute-done | bytes 1568 | tf_op jit(solution)/shard_map/ppermute | solution.py:25
  187.5 3.1 %collective-permute-done.21 = f32[3,6,1,32]{3,2,1,0:T(1,128)S(1)} collective-permute-done((f32[3,6,1,32]{3,2,1,0:T(1,128)S(1)}, f32[3,6,1,32]{3,2,1,0:T(1,128)S(1)}, u32[]{:S(2)}, u32[]{:S(2)}) %collective-permute-start.21) | collective-permute-done | bytes 2336 | tf_op jit(solution)/shard_map/ppermute | solution.py:25
  190.8 5.5 %collective-permute-start.22 = (f32[3,6,6,1]{3,2,1,0:T(8,128)S(1)}, f32[3,6,6,1]{3,2,1,0:T(8,128)S(1)}, u32[]{:S(2)}, u32[]{:S(2)}) collective-permute-start(f32[3,6,6,1]{3,2,1,0:T(8,128)S(1)} %get-tuple-element.96), channel_id=1, source_target_pairs={{0,1},{1,2},{2,3},{3,4},{4,5},{5,6},{6,7},{8,9},{9,10},{10,11},{11... | collective-permute-start | bytes 1304 | tf_op jit(solution)/shard_map/ppermute | solution.py:22
  198.2 3.7 %collective-permute-done.23 = f32[3,6,6,1]{3,2,1,0:T(8,128)S(1)} collective-permute-done((f32[3,6,6,1]{3,2,1,0:T(8,128)S(1)}, f32[3,6,6,1]{3,2,1,0:T(8,128)S(1)}, u32[]{:S(2)}, u32[]{:S(2)}) %collective-permute-start.23) | collective-permute-done | bytes 464 | tf_op jit(solution)/shard_map/ppermute | solution.py:25
  213.0 18.3 %all_to_all.40 = f32[64,6,16]{2,1,0:T(8,128)S(1)} all-to-all(f32[64,6,16]{2,1,0:T(8,128)S(1)} %constant_dynamic-update-slice_fusion.70), channel_id=1, replica_groups=mesh['gx'=8,'gy'=8,'gz'=8] {'gy','gz'}, dimensions={0} | all-to-all | bytes 49152 | tf_op jit(solution)/shard_map/all_to_all | solution.py:264
  (468 shorter events, 73.2 us)
Async XLA Ops:
  3.1 32.1 %all-to-all-start = ((f32[1,64,2]{2,0,1:T(1,128)}), f32[1,64,2]{2,0,1:T(1,128)S(1)}, u32[]{:S(2)}, u32[]{:S(2)}) async-start(f32[1,64,2]{2,0,1:T(1,128)} %bitcast.2), calls=%async_computation | async-start | bytes 65536 | tf_op jit(solution)/shard_map/all_to_all | solution.py:239
  14.7 82.5 %collective-permute-start = (bf16[2,5,16,128]{3,2,1,0:T(8,128)(2,1)S(1)}, bf16[2,5,16,128]{3,2,1,0:T(8,128)(2,1)S(1)}, u32[]{:S(2)}, u32[]{:S(2)}) collective-permute-start(bf16[2,5,16,128]{3,2,1,0:T(8,128)(2,1)S(1)} %get-tuple-element.88), channel_id=1, source_target_pairs={{0,64},{64,128},{128,192},{192,256},{256,320},{320,384},{384,448},... | collective-permute-start | bytes 122888 | tf_op jit(solution)/shard_map/ppermute | solution.py:22
  20.9 8.7 %collective-permute-start.6 = (bf16[2,16,128]{2,1,0:T(8,128)(2,1)S(1)}, bf16[2,16,128]{2,1,0:T(8,128)(2,1)S(1)}, u32[]{:S(2)}, u32[]{:S(2)}) collective-permute-start(bf16[2,16,128]{2,1,0:T(8,128)(2,1)S(1)} %get-tuple-element.102), channel_id=1, source_target_pairs={{0,64},{64,128},{128,192},{192,256},{256,320},{320,384},{384,448},... | collective-permute-start | bytes 24584 | tf_op jit(solution)/shard_map/ppermute | solution.py:22
  24.0 5.6 %collective-permute-start.7 = (bf16[2,16,128]{2,1,0:T(8,128)(2,1)S(1)}, bf16[2,16,128]{2,1,0:T(8,128)(2,1)S(1)}, u32[]{:S(2)}, u32[]{:S(2)}) collective-permute-start(bf16[2,16,128]{2,1,0:T(8,128)(2,1)S(1)} %get-tuple-element.103), channel_id=1, source_target_pairs={{64,0},{128,64},{192,128},{256,192},{320,256},{384,320},{448,384},... | collective-permute-start | bytes 24584 | tf_op jit(solution)/shard_map/ppermute | solution.py:25
  29.7 21.5 %collective-permute-start.8 = (bf16[20,2,128]{2,1,0:T(2,128)(2,1)S(1)}, bf16[20,2,128]{2,1,0:T(2,128)(2,1)S(1)}, u32[]{:S(2)}, u32[]{:S(2)}) collective-permute-start(bf16[20,2,128]{2,1,0:T(2,128)(2,1)S(1)} %get-tuple-element.92), channel_id=1, source_target_pairs={{0,8},{8,16},{16,24},{24,32},{32,40},{40,48},{48,56},{1,9},{9,17},... | collective-permute-start | bytes 30728 | tf_op jit(solution)/shard_map/ppermute | solution.py:22
  33.0 18.2 %collective-permute-start.9 = (bf16[20,2,128]{2,1,0:T(2,128)(2,1)S(1)}, bf16[20,2,128]{2,1,0:T(2,128)(2,1)S(1)}, u32[]{:S(2)}, u32[]{:S(2)}) collective-permute-start(bf16[20,2,128]{2,1,0:T(2,128)(2,1)S(1)} %get-tuple-element.93), channel_id=1, source_target_pairs={{8,0},{16,8},{24,16},{32,24},{40,32},{48,40},{56,48},{9,1},{17,9},... | collective-permute-start | bytes 30728 | tf_op jit(solution)/shard_map/ppermute | solution.py:25
  35.2 25.5 %all-to-all-start.1 = ((f32[3,64,16]{2,0,1:T(4,128)}), f32[3,64,16]{2,0,1:T(4,128)S(1)}, u32[]{:S(2)}, u32[]{:S(2)}) async-start(f32[3,64,16]{2,0,1:T(4,128)} %copy.528), calls=%async_computation.1 | async-start | bytes 262144 | tf_op jit(solution)/shard_map/all_to_all | solution.py:236
  61.4 10.2 %collective-permute-start.12 = (f32[3,1,4,32]{3,2,1,0:T(4,128)S(1)}, f32[3,1,4,32]{3,2,1,0:T(4,128)S(1)}, u32[]{:S(2)}, u32[]{:S(2)}) collective-permute-start(f32[3,1,4,32]{3,2,1,0:T(4,128)S(1)} %get-tuple-element.115), channel_id=1, source_target_pairs={{0,64},{64,128},{128,192},{192,256},{256,320},{320,384},{384,448},... | collective-permute-start | bytes 4616 | tf_op jit(solution)/shard_map/ppermute | solution.py:22
  65.1 14.8 %collective-permute-start.10 = (bf16[20,20,2]{2,1,0:T(8,128)(2,1)S(1)}, bf16[20,20,2]{2,1,0:T(8,128)(2,1)S(1)}, u32[]{:S(2)}, u32[]{:S(2)}) collective-permute-start(bf16[20,20,2]{2,1,0:T(8,128)(2,1)S(1)} %get-tuple-element.90), channel_id=1, source_target_pairs={{0,1},{1,2},{2,3},{3,4},{4,5},{5,6},{6,7},{8,9},{9,10},{10,11},{11... | collective-permute-start | bytes 4808 | tf_op jit(solution)/shard_map/ppermute | solution.py:22
  67.7 14.6 %collective-permute-start.11 = (bf16[20,20,2]{2,1,0:T(8,128)(2,1)S(1)}, bf16[20,20,2]{2,1,0:T(8,128)(2,1)S(1)}, u32[]{:S(2)}, u32[]{:S(2)}) collective-permute-start(bf16[20,20,2]{2,1,0:T(8,128)(2,1)S(1)} %get-tuple-element.91), channel_id=1, source_target_pairs={{1,0},{2,1},{3,2},{4,3},{5,4},{6,5},{7,6},{9,8},{10,9},{11,10},{12... | collective-permute-start | bytes 4808 | tf_op jit(solution)/shard_map/ppermute | solution.py:25
  69.7 5.6 %collective-permute-start.13 = (f32[3,1,4,32]{3,2,1,0:T(4,128)S(1)}, f32[3,1,4,32]{3,2,1,0:T(4,128)S(1)}, u32[]{:S(2)}, u32[]{:S(2)}) collective-permute-start(f32[3,1,4,32]{3,2,1,0:T(4,128)S(1)} %get-tuple-element.114), channel_id=1, source_target_pairs={{64,0},{128,64},{192,128},{256,192},{320,256},{384,320},{448,384},... | collective-permute-start | bytes 4616 | tf_op jit(solution)/shard_map/ppermute | solution.py:25
  75.3 7.6 %collective-permute-start.14 = (f32[3,6,1,32]{3,2,1,0:T(1,128)S(1)}, f32[3,6,1,32]{3,2,1,0:T(1,128)S(1)}, u32[]{:S(2)}, u32[]{:S(2)}) collective-permute-start(f32[3,6,1,32]{3,2,1,0:T(1,128)S(1)} %get-tuple-element.110), channel_id=1, source_target_pairs={{0,8},{8,16},{16,24},{24,32},{32,40},{40,48},{48,56},{1,9},{9,17},... | collective-permute-start | bytes 6920 | tf_op jit(solution)/shard_map/ppermute | solution.py:22
  77.8 5.0 %collective-permute-start.15 = (f32[3,6,1,32]{3,2,1,0:T(1,128)S(1)}, f32[3,6,1,32]{3,2,1,0:T(1,128)S(1)}, u32[]{:S(2)}, u32[]{:S(2)}) collective-permute-start(f32[3,6,1,32]{3,2,1,0:T(1,128)S(1)} %get-tuple-element.111), channel_id=1, source_target_pairs={{8,0},{16,8},{24,16},{32,24},{40,32},{48,40},{56,48},{9,1},{17,9},... | collective-permute-start | bytes 6920 | tf_op jit(solution)/shard_map/ppermute | solution.py:25
  79.9 17.3 %collective-permute-start.1 = (bf16[2,5,16,128]{3,2,1,0:T(8,128)(2,1)S(1)}, bf16[2,5,16,128]{3,2,1,0:T(8,128)(2,1)S(1)}, u32[]{:S(2)}, u32[]{:S(2)}) collective-permute-start(bf16[2,5,16,128]{3,2,1,0:T(8,128)(2,1)S(1)} %get-tuple-element.89), channel_id=1, source_target_pairs={{64,0},{128,64},{192,128},{256,192},{320,256},{384,320},{448,384},... | collective-permute-start | bytes 122888 | tf_op jit(solution)/shard_map/ppermute | solution.py:25
  83.0 7.9 %collective-permute-start.16 = (f32[3,6,6,1]{3,2,1,0:T(8,128)S(1)}, f32[3,6,6,1]{3,2,1,0:T(8,128)S(1)}, u32[]{:S(2)}, u32[]{:S(2)}) collective-permute-start(f32[3,6,6,1]{3,2,1,0:T(8,128)S(1)} %get-tuple-element.100), channel_id=1, source_target_pairs={{0,1},{1,2},{2,3},{3,4},{4,5},{5,6},{6,7},{8,9},{9,10},{10,11},{11... | collective-permute-start | bytes 1304 | tf_op jit(solution)/shard_map/ppermute | solution.py:22
  88.6 5.7 %collective-permute-start.17 = (f32[3,6,6,1]{3,2,1,0:T(8,128)S(1)}, f32[3,6,6,1]{3,2,1,0:T(8,128)S(1)}, u32[]{:S(2)}, u32[]{:S(2)}) collective-permute-start(f32[3,6,6,1]{3,2,1,0:T(8,128)S(1)} %get-tuple-element.101), channel_id=1, source_target_pairs={{1,0},{2,1},{3,2},{4,3},{5,4},{6,5},{7,6},{9,8},{10,9},{11,10},{12... | collective-permute-start | bytes 1304 | tf_op jit(solution)/shard_map/ppermute | solution.py:25
  97.3 5.5 %collective-permute-start.2 = (bf16[2,26,5,128]{3,2,1,0:T(8,128)(2,1)S(1)}, bf16[2,26,5,128]{3,2,1,0:T(8,128)(2,1)S(1)}, u32[]{:S(2)}, u32[]{:S(2)}) collective-permute-start(bf16[2,26,5,128]{3,2,1,0:T(8,128)(2,1)S(1)} %get-tuple-element.78), channel_id=1, source_target_pairs={{0,8},{8,16},{16,24},{24,32},{32,40},{40,48},{48,56},{1,9},{9,17},... | collective-permute-start | bytes 199688 | tf_op jit(solution)/shard_map/ppermute | solution.py:22
  101.1 5.4 %collective-permute-start.3 = (bf16[2,26,5,128]{3,2,1,0:T(8,128)(2,1)S(1)}, bf16[2,26,5,128]{3,2,1,0:T(8,128)(2,1)S(1)}, u32[]{:S(2)}, u32[]{:S(2)}) collective-permute-start(bf16[2,26,5,128]{3,2,1,0:T(8,128)(2,1)S(1)} %get-tuple-element.79), channel_id=1, source_target_pairs={{8,0},{16,8},{24,16},{32,24},{40,32},{48,40},{56,48},{9,1},{17,9},... | collective-permute-start | bytes 199688 | tf_op jit(solution)/shard_map/ppermute | solution.py:25
  107.8 9.5 %collective-permute-start.4 = (bf16[2,26,26,5]{3,2,1,0:T(8,128)(2,1)}, bf16[2,26,26,5]{3,2,1,0:T(8,128)(2,1)}, u32[]{:S(2)}, u32[]{:S(2)}) collective-permute-start(bf16[2,26,26,5]{3,2,1,0:T(8,128)(2,1)} %get-tuple-element.64), channel_id=1, source_target_pairs={{0,1},{1,2},{2,3},{3,4},{4,5},{5,6},{6,7},{8,9},{9,10},{10,11},{11... | collective-permute-start | bytes 40568 | tf_op jit(solution)/shard_map/ppermute | solution.py:22
  112.0 9.8 %collective-permute-start.5 = (bf16[2,26,26,5]{3,2,1,0:T(8,128)(2,1)}, bf16[2,26,26,5]{3,2,1,0:T(8,128)(2,1)}, u32[]{:S(2)}, u32[]{:S(2)}) collective-permute-start(bf16[2,26,26,5]{3,2,1,0:T(8,128)(2,1)} %get-tuple-element.65), channel_id=1, source_target_pairs={{1,0},{2,1},{3,2},{4,3},{5,4},{6,5},{7,6},{9,8},{10,9},{11,10},{12... | collective-permute-start | bytes 40568 | tf_op jit(solution)/shard_map/ppermute | solution.py:25
  173.4 6.8 %collective-permute-start.18 = (f32[3,1,4,32]{3,2,1,0:T(4,128)S(1)}, f32[3,1,4,32]{3,2,1,0:T(4,128)S(1)}, u32[]{:S(2)}, u32[]{:S(2)}) collective-permute-start(f32[3,1,4,32]{3,2,1,0:T(4,128)S(1)} %get-tuple-element.113), channel_id=1, source_target_pairs={{0,64},{64,128},{128,192},{192,256},{256,320},{320,384},{384,448},... | collective-permute-start | bytes 4616 | tf_op jit(solution)/shard_map/ppermute | solution.py:22
  178.3 5.6 %collective-permute-start.19 = (f32[3,1,4,32]{3,2,1,0:T(4,128)S(1)}, f32[3,1,4,32]{3,2,1,0:T(4,128)S(1)}, u32[]{:S(2)}, u32[]{:S(2)}) collective-permute-start(f32[3,1,4,32]{3,2,1,0:T(4,128)S(1)} %get-tuple-element.112), channel_id=1, source_target_pairs={{64,0},{128,64},{192,128},{256,192},{320,256},{384,320},{448,384},... | collective-permute-start | bytes 4616 | tf_op jit(solution)/shard_map/ppermute | solution.py:25
  190.8 7.4 %collective-permute-start.22 = (f32[3,6,6,1]{3,2,1,0:T(8,128)S(1)}, f32[3,6,6,1]{3,2,1,0:T(8,128)S(1)}, u32[]{:S(2)}, u32[]{:S(2)}) collective-permute-start(f32[3,6,6,1]{3,2,1,0:T(8,128)S(1)} %get-tuple-element.96), channel_id=1, source_target_pairs={{0,1},{1,2},{2,3},{3,4},{4,5},{5,6},{6,7},{8,9},{9,10},{10,11},{11... | collective-permute-start | bytes 1304 | tf_op jit(solution)/shard_map/ppermute | solution.py:22
  196.2 5.7 %collective-permute-start.23 = (f32[3,6,6,1]{3,2,1,0:T(8,128)S(1)}, f32[3,6,6,1]{3,2,1,0:T(8,128)S(1)}, u32[]{:S(2)}, u32[]{:S(2)}) collective-permute-start(f32[3,6,6,1]{3,2,1,0:T(8,128)S(1)} %get-tuple-element.97), channel_id=1, source_target_pairs={{1,0},{2,1},{3,2},{4,3},{5,4},{6,5},{7,6},{9,8},{10,9},{11,10},{12... | collective-permute-start | bytes 1304 | tf_op jit(solution)/shard_map/ppermute | solution.py:25
  (49 other events, 863.0 us)
